TPU v7x, 32 devices: a whole 2x2x4 slice. The times are simulated.
32 devices in a mesh: cuts: 2 (over x), mode: 16 (over z, y, core).
Axes of the slice: x: 2, y: 2, z: 4, core: 2. Of those that a mesh axis runs over, the one named last changes fastest.
Arguments:
- stem_blocks: bfloat16 [2, 4096, 2, 256], P('cuts', 'mode'), may hold values from -6 to 6
- w1_table: bfloat16 [8, 2, 256, 256], replicated, may hold values from -0.25 to 0.25
- w2_table: bfloat16 [8, 2, 256, 256], replicated, may hold values from -0.125 to 0.125
- slice_ids: int32 [2, 2, 2], P('cuts'), may hold values from 0 to 7, as said below
- mode_perm: int32 [256], replicated, may hold values from 0 to 255, each once
Outputs:
- amplitudes: float32 [256, 16, 2, 256], P('mode', 'cuts')
Inputs may be any that keep to these rules, and one draw needn't show every extreme that they name: For each stem block b, the 2 values slice_ids[:,b,0] are distinct, and so are the 2 values slice_ids[:,b,1]. `mode_perm`: each column appears once.
All inputs are finite; a program needn't handle non-finite values.
Results may differ from a plain program's by a relative error of at most 0.0029.
Values may be sent and summed in bfloat16 or wider, within the bound.
No kernel may reach another device: no remote copies, remote signals or barrier semaphores. Data moves between devices by JAX's collectives and lax.ppermute only.
A program may use at most 64 MiB of HBM per device.

v0:
```python
import jax
import jax.numpy as jnp
from jax import lax
from jax.sharding import PartitionSpec as P


def broadcast(block, axis, source):
    block = jnp.where(lax.axis_index(axis) == source, block, jnp.zeros_like(block))
    return lax.psum(block, axis)


def widen_first(entry):
    real_part, imag_part = (entry[0], entry[1])
    upper = jnp.concatenate([real_part, imag_part], axis=1)
    lower = jnp.concatenate([-imag_part, real_part], axis=1)
    return jnp.concatenate([upper, lower], axis=0)


def widen_second(entry):
    real_part, imag_part = (entry[0], entry[1])
    first_row = jnp.concatenate([real_part, imag_part], axis=1)
    second_row = jnp.concatenate([-imag_part, real_part], axis=1)
    return jnp.stack([first_row, second_row], axis=0)


def second_step(exchanged, weight_two, contract_cols, free_cols):
    block_count, mode_count, piece_rows, _ = exchanged.shape
    pieces = exchanged.reshape(block_count, mode_count, piece_rows, 2, contract_cols, free_cols)
    wide_out = weight_two.shape[3]
    shaped = weight_two.reshape(block_count, 2, mode_count, contract_cols, wide_out)
    return jnp.einsum("nhqpcs,nphco->qso", pieces, shaped, preferred_element_type=jnp.float32)


def on_device(stem_blocks, w1_table, w2_table, slice_ids, mode_perm):
    mode_count = lax.axis_size("mode")
    row_count = stem_blocks.shape[1]
    stem_width = stem_blocks.shape[3]
    mid_width = w1_table.shape[3]
    inner_width = w2_table.shape[2]
    out_width = w2_table.shape[3]
    piece_rows = row_count // mode_count
    contract_cols = inner_width // mode_count
    free_cols = mid_width // contract_cols
    block_count = slice_ids.shape[1]
    first_all = jax.vmap(widen_first)(jnp.take(w1_table, mode_perm, axis=3))
    second_all = jax.vmap(widen_second)(w2_table)
    own_slices = slice_ids[0]
    begin = jnp.zeros((piece_rows, free_cols, 2 * out_width), jnp.float32)

    def one_block(block_index, running):
        stem_part = broadcast(stem_blocks[0], "cuts", block_index)
        slice_pair = own_slices[block_index]
        weight_one = lax.dynamic_index_in_dim(first_all, slice_pair[0], 0, keepdims=False)
        product = jnp.dot(
            stem_part.reshape(row_count, 2 * stem_width),
            weight_one,
            preferred_element_type=jnp.float32,
        ).astype(jnp.bfloat16)
        exchanged = lax.all_to_all(
            product[None, None], "mode", split_axis=2, concat_axis=1, tiled=True
        )
        weight_two = lax.dynamic_index_in_dim(second_all, slice_pair[1], 0, keepdims=True)
        return running + second_step(exchanged, weight_two, contract_cols, free_cols)

    amplitude = lax.fori_loop(0, block_count, one_block, begin)
    summed = lax.psum_scatter(amplitude, "cuts", scatter_dimension=1, tiled=True)
    return summed.reshape(piece_rows, summed.shape[1], 2, out_width)


def solution(mesh):
    placed = (P("cuts", "mode", None, None), P(), P(), P("cuts", None, None), P())
    return jax.shard_map(
        on_device,
        mesh=mesh,
        in_specs=placed,
        out_specs=P("mode", "cuts", None, None),
        check_vma=False,
    )
```

profile of v0, /device:TPU:0, one launch (start us, length us, event | category | flops | bytes accessed | tf_op | source)
XLA Modules:
  0.0 173.1 jit_solution(13787529332660151836)
XLA Ops:
  7.4 3.2 %slice_bitcast_fusion.2 = (bf16[8,256,256]{2,1,0:T(8,128)(2,1)}, bf16[8,256,256]{2,1,0:T(8,128)(2,1)}) fusion(bf16[8,2,256,256]{3,2,1,0:T(8,128)(2,1)} %param.9), kind=kLoop, calls=%fused_computation.19 | loop fusion | bytes 4194304 | tf_op jit(solution)/shard_map/vmap()/squeeze | solution.py:20
  10.6 1.1 fusion.6
  11.7 0.9 copy-done.6
  12.6 3.1 %copy.29 = bf16[8,2,256,256]{2,0,3,1:T(8,128)(2,1)} copy(bf16[8,2,256,256]{3,2,1,0:T(8,128)(2,1)S(1)} %copy-done.6) | data formatting | bytes 4194304 | tf_op args[1]
  15.7 2.4 %gather_fusion = bf16[256,8,2,256]{3,1,2,0:T(8,128)(2,1)S(1)} fusion(bf16[8,2,256,256]{2,0,3,1:T(8,128)(2,1)} %copy.29, s32[1024]{0:T(1024)S(1)} %pad_clamp_fusion), kind=kCustom, calls=%fused_computation | custom fusion | bytes 4195328 | tf_op jit(solution)/shard_map/jit(_take)/gather | solution.py:45
  18.1 0.9 select_bitcast_fusion
  19.0 1.1 slice_bitcast_fusion
  20.2 13.0 %maximum_maximum_fusion = bf16[8,512,512]{1,0,2:T(8,128)(2,1)} fusion(bf16[8,256,256]{1,0,2:T(8,128)(2,1)} %get-tuple-element.171, bf16[8,256,256]{1,0,2:T(8,128)(2,1)S(1)} %fusion.7, bf16[8,256,256]{1,0,2:T(8,128)(2,1)S(1)} %get-tuple-element.170), kind=kLoop, calls=%fused_computation.12 | loop fusion | flops 16777216 | bytes 7340032 | tf_op jit(solution)/shard_map/vmap()/concatenate | solution.py:16
  33.3 7.7 %copy.34 = bf16[8,512,512]{2,1,0:T(8,128)(2,1)} copy(bf16[8,512,512]{1,0,2:T(8,128)(2,1)} %maximum_maximum_fusion) | data formatting | bytes 8388608
  41.0 1.9 %maximum_bitcast_fusion.1 = (bf16[1,8,256,512]{3,2,0,1:T(8,128)(2,1)S(1)}, bf16[1,8,256,512]{3,2,0,1:T(8,128)(2,1)S(1)}) fusion(bf16[8,256,256]{2,1,0:T(8,128)(2,1)S(1)} %copy-done.5, bf16[8,256,256]{2,1,0:T(8,128)(2,1)} %get-tuple-element.169, bf16[8,256,256]{2,1,0:T(8,128)(2,1)S(1)} %copy-done.4), kind=kLoop, calls=%fused_computation.14 | loop fusion | flops 8388608 | bytes 7340032 | tf_op jit(solution)/shard_map/vmap()/stack | solution.py:23
  42.9 2.3 %maximum_bitcast_fusion = bf16[8,2,256,512]{3,2,1,0:T(8,128)(2,1)} fusion(bf16[1,8,256,512]{3,2,0,1:T(8,128)(2,1)S(1)} %get-tuple-element.173, bf16[1,8,256,512]{3,2,0,1:T(8,128)(2,1)S(1)} %get-tuple-element.172), kind=kLoop, calls=%fused_computation.13 | loop fusion | flops 2097152 | bytes 8388608 | tf_op jit(solution)/shard_map/vmap()/transpose | solution.py:46
  45.3 104.0 %while.14 = (s32[]{:T(128)}, f32[16,16,512]{2,1,0:T(8,128)S(1)}, bf16[1,256,2,256]{3,2,1,0:T(2,128)(2,1)S(1)}, s32[2,2]{1,0:T(2,128)S(1)}, bf16[8,512,512]{2,1,0...) while((s32[]{:T(128)}, f32[16,16,512]{2,1,0:T(8,128)S(1)}, ...), condition=%wide.region_2.3_spmd.clone, body=%wide.region_0.0_spmd.clone.sunk | while | flops 269090816 | bytes 11534731 | solution.py:65
  48.9 25.5 %all-reduce.2.cloned.1.call-done = bf16[256,512]{1,0:T(8,128)(2,1)} async-done(((bf16[256,512]{1,0:T(8,128)(2,1)}), bf16[256,512]{1,0:T(8,128)(2,1)}) %all-reduce.2.cloned.1.call-update) | async-done | bytes 262160 | tf_op jit(solution)/shard_map/while/body/eval_jaxpr/psum | solution.py:9
  74.4 1.4 fusion.23
  76.7 2.2 %reduce.6 = bf16[256,512]{1,0:T(8,128)(2,1)S(1)} reduce(bf16[256,1,1,512]{3,2,1,0:T(2,128)(2,1)S(1)} %bitcast.79, bf16[]{:T(256)} %broadcast.40), dimensions={1,2}, to_apply=%bitcast.54.reduce_sub_computation | reduce | bytes 524290 | tf_op jit(solution)/shard_map/while
  79.0 0.9 reshape.66
  79.8 5.6 %all-to-all-start = ((bf16[16,2,4096]{2,1,0:T(2,128)(2,1)}), bf16[16,2,4096]{2,1,0:T(2,128)(2,1)S(1)}, u32[]{:S(2)}, u32[]{:S(2)}) async-start(bf16[16,2,4096]{2,1,0:T(2,128)(2,1)} %reshape.66), calls=%async_computation | async-start | bytes 524288 | tf_op jit(solution)/shard_map/while/body/eval_jaxpr/all_to_all | solution.py:59
  87.5 1.1 constant_dynamic-slice_fusion.5
  88.6 6.9 %all-to-all-done = bf16[16,2,4096]{2,1,0:T(2,128)(2,1)S(1)} async-done(((bf16[16,2,4096]{2,1,0:T(2,128)(2,1)}), bf16[16,2,4096]{2,1,0:T(2,128)(2,1)S(1)}, u32[]{:S(2)}, u32[]{:S(2)}) %all-to-all-start) | async-done | bytes 262176 | tf_op jit(solution)/shard_map/while/body/eval_jaxpr/all_to_all | solution.py:59
  95.8 1.5 bitcast_reduce_fusion.2
  97.3 1.7 reshape.68
  103.5 20.2 %all-reduce.2.cloned.1.call-done = bf16[256,512]{1,0:T(8,128)(2,1)} async-done(((bf16[256,512]{1,0:T(8,128)(2,1)}), bf16[256,512]{1,0:T(8,128)(2,1)}) %all-reduce.2.cloned.1.call-update) | async-done | bytes 262160 | tf_op jit(solution)/shard_map/while/body/eval_jaxpr/psum | solution.py:9
  123.7 1.4 fusion.23
  126.1 2.2 %reduce.6 = bf16[256,512]{1,0:T(8,128)(2,1)S(1)} reduce(bf16[256,1,1,512]{3,2,1,0:T(2,128)(2,1)S(1)} %bitcast.79, bf16[]{:T(256)} %broadcast.40), dimensions={1,2}, to_apply=%bitcast.54.reduce_sub_computation | reduce | bytes 524290 | tf_op jit(solution)/shard_map/while
  128.3 0.9 reshape.66
  129.2 5.6 %all-to-all-start = ((bf16[16,2,4096]{2,1,0:T(2,128)(2,1)}), bf16[16,2,4096]{2,1,0:T(2,128)(2,1)S(1)}, u32[]{:S(2)}, u32[]{:S(2)}) async-start(bf16[16,2,4096]{2,1,0:T(2,128)(2,1)} %reshape.66), calls=%async_computation | async-start | bytes 524288 | tf_op jit(solution)/shard_map/while/body/eval_jaxpr/all_to_all | solution.py:59
  136.9 1.1 constant_dynamic-slice_fusion.5
  138.0 6.9 %all-to-all-done = bf16[16,2,4096]{2,1,0:T(2,128)(2,1)S(1)} async-done(((bf16[16,2,4096]{2,1,0:T(2,128)(2,1)}), bf16[16,2,4096]{2,1,0:T(2,128)(2,1)S(1)}, u32[]{:S(2)}, u32[]{:S(2)}) %all-to-all-start) | async-done | bytes 262176 | tf_op jit(solution)/shard_map/while/body/eval_jaxpr/all_to_all | solution.py:59
  145.1 1.5 bitcast_reduce_fusion.2
  146.6 1.7 reshape.68
  150.1 13.7 %reduce-scatter.2.cloned.1.call-done = f32[16,8,512]{2,1,0:T(8,128)} async-done(((f32[16,16,512]{2,1,0:T(8,128)}), f32[16,8,512]{2,1,0:T(8,128)}) %reduce-scatter.2.cloned.1.call-update) | async-done | bytes 262160 | tf_op jit(solution)/shard_map/reduce_scatter | solution.py:66
  163.8 1.8 %reshape.44 = f32[16,8,2,256]{3,2,1,0:T(2,128)} reshape(f32[16,8,512]{2,1,0:T(8,128)} %reduce-scatter.2.cloned.1.call-done) | data formatting | bytes 524288 | tf_op jit(solution)/shard_map/reshape | solution.py:67
  (46 shorter events, 8.5 us)
Async XLA Ops:
  7.4 3.2 %copy-start.3 = (bf16[8,2,256,256]{3,2,1,0:T(8,128)(2,1)S(1)}, bf16[8,2,256,256]{3,2,1,0:T(8,128)(2,1)}, u32[]{:S(2)}) copy-start(bf16[8,2,256,256]{3,2,1,0:T(8,128)(2,1)} %param.9) | copy-start | bytes 6291460
  7.4 4.3 %copy-start.7 = (s32[256]{0:T(256)S(1)}, s32[256]{0:T(256)}, u32[]{:S(2)}) copy-start(s32[256]{0:T(256)} %param.11) | copy-start | bytes 3076
  10.6 2.0 %copy-start.6 = (bf16[8,2,256,256]{3,2,1,0:T(8,128)(2,1)S(1)}, bf16[8,2,256,256]{3,2,1,0:T(8,128)(2,1)}, u32[]{:S(2)}) copy-start(bf16[8,2,256,256]{3,2,1,0:T(8,128)(2,1)} %param.8) | copy-start | bytes 6291460
  33.3 7.7 %copy-start.4 = (bf16[8,256,256]{2,1,0:T(8,128)(2,1)S(1)}, bf16[8,256,256]{2,1,0:T(8,128)(2,1)}, u32[]{:S(2)}) copy-start(bf16[8,256,256]{2,1,0:T(8,128)(2,1)} %fusion.6) | copy-start | bytes 3145732
  33.3 7.7 %copy-start.5 = (bf16[8,256,256]{2,1,0:T(8,128)(2,1)S(1)}, bf16[8,256,256]{2,1,0:T(8,128)(2,1)}, u32[]{:S(2)}) copy-start(bf16[8,256,256]{2,1,0:T(8,128)(2,1)} %get-tuple-element.168) | copy-start | bytes 3145732
  42.9 2.4 %copy-start.1 = (bf16[1,256,2,256]{3,2,1,0:T(2,128)(2,1)S(1)}, bf16[1,256,2,256]{3,2,1,0:T(2,128)(2,1)}, u32[]{:S(2)}) copy-start(bf16[1,256,2,256]{3,2,1,0:T(2,128)(2,1)} %param.7) | copy-start | bytes 786436
  42.9 2.4 %copy-start.8 = (s32[1,2,2]{2,1,0:T(2,128)S(1)}, s32[1,2,2]{2,1,0:T(2,128)}, u32[]{:S(2)}) copy-start(s32[1,2,2]{2,1,0:T(2,128)} %param.10) | copy-start | bytes 52
  45.3 29.1 %all-reduce.2.cloned.1.call-start = ((), (), s32[]{:S(2)}) async-start(), calls=%async_computation.3 | async-start | bytes 524288 | tf_op jit(solution)/shard_map/while/body/eval_jaxpr/psum | solution.py:9
  79.8 15.7 %all-to-all-start = ((bf16[16,2,4096]{2,1,0:T(2,128)(2,1)}), bf16[16,2,4096]{2,1,0:T(2,128)(2,1)S(1)}, u32[]{:S(2)}, u32[]{:S(2)}) async-start(bf16[16,2,4096]{2,1,0:T(2,128)(2,1)} %reshape.66), calls=%async_computation | async-start | bytes 524288 | tf_op jit(solution)/shard_map/while/body/eval_jaxpr/all_to_all | solution.py:59
  99.0 1.0 copy-start.2
  99.9 23.8 %all-reduce.2.cloned.1.call-start = ((), (), s32[]{:S(2)}) async-start(), calls=%async_computation.3 | async-start | bytes 524288 | tf_op jit(solution)/shard_map/while/body/eval_jaxpr/psum | solution.py:9
  129.2 15.7 %all-to-all-start = ((bf16[16,2,4096]{2,1,0:T(2,128)(2,1)}), bf16[16,2,4096]{2,1,0:T(2,128)(2,1)S(1)}, u32[]{:S(2)}, u32[]{:S(2)}) async-start(bf16[16,2,4096]{2,1,0:T(2,128)(2,1)} %reshape.66), calls=%async_computation | async-start | bytes 524288 | tf_op jit(solution)/shard_map/while/body/eval_jaxpr/all_to_all | solution.py:59
  148.3 1.0 copy-start.2
  149.3 0.8 copy-start
  149.3 14.5 %reduce-scatter.2.cloned.1.call-start = ((), (), s32[]{:S(2)}) async-start(), calls=%async_computation.2 | async-start | bytes 786432 | tf_op jit(solution)/shard_map/reduce_scatter | solution.py:66
Sparse Core Ops, SparseCore 0:
  48.5 25.8 all-reduce.1
  103.1 20.5 all-reduce.1
Sparse Core Ops, SparseCore 1:
  152.0 11.8 reduce-scatter.1
where the time goes:
time: 174 us; the launch traced here: 173 us
  waiting for transfers between devices  73.3 us (42%)
  local copies, waits for them, and re-layouts  37 us (21%)
  other arithmetic  24.2 us (14%)
  between operations  14.9 us (9%)
  starting transfers between devices  11.3 us (6%)
  loops' own time  8.19 us (5%)
  matrix products  4.28 us (2%)
    psum x2, waiting for transfers between devices, broadcast(): return lax.psum(block, axis)  45.7 us
    all_to_all x2, waiting for transfers between devices, one_block(): lax.all_to_all(product[None, None], 'mode', split_axis=2, concat_axis=1,...  13.8 us
    reduce_scatter x1, waiting for transfers between devices, on_device(): lax.psum_scatter(amplitude, 'cuts', scatter_dimension=1, tiled=True)  13.7 us
    concatenate x1, other arithmetic, widen_first(): return jnp.concatenate([upper, lower], axis=0)  13 us
    unnamed x18, local copies, waits for them, and re-layouts  12.5 us
    all_to_all x2, starting transfers between devices, one_block(): lax.all_to_all(product[None, None], 'mode', split_axis=2, concat_axis=1,...  11.2 us
    another operation x1, loops' own time, on_device(): amplitude = lax.fori_loop(0, block_count, one_block, begin)  8.19 us
    while x12, local copies, waits for them, and re-layouts  5.23 us
  transfers between devices with their start and end apart: 5, of which 5 were waited for; matrix products, arithmetic and copies ran while one was open for 2% of the time, Pallas kernels for 0%

commit v1 on v0

--- a/solution.py
+++ b/solution.py
@@ -2,6 +2,22 @@
 import jax.numpy as jnp
 from jax import lax
 from jax.sharding import PartitionSpec as P
+
+
+def pairwise_exchange(x, axis, split, join):
+    ways, here = (lax.axis_size(axis), lax.axis_index(axis))
+    width = x.shape[split] // ways
+    shape = list(x.shape)
+    shape[split] = width
+    height = shape[join]
+    shape[join] = height * ways
+    full = jnp.zeros(shape, x.dtype)
+    for mask in range(ways):
+        part = lax.dynamic_slice_in_dim(x, (here ^ mask) * width, width, axis=split)
+        if mask:
+            part = lax.ppermute(part, axis, [(d, d ^ mask) for d in range(ways)])
+        full = lax.dynamic_update_slice_in_dim(full, part, (here ^ mask) * height, axis=join)
+    return full
 
 
 def broadcast(block, axis, source):
@@ -56,9 +72,7 @@
             weight_one,
             preferred_element_type=jnp.float32,
         ).astype(jnp.bfloat16)
-        exchanged = lax.all_to_all(
-            product[None, None], "mode", split_axis=2, concat_axis=1, tiled=True
-        )
+        exchanged = pairwise_exchange(product[None, None], "mode", 2, 1)
         weight_two = lax.dynamic_index_in_dim(second_all, slice_pair[1], 0, keepdims=True)
         return running + second_step(exchanged, weight_two, contract_cols, free_cols)
 

time: 174 us -> 182 us (1.046)
  starting transfers between devices: 11.3 us -> 41.2 us
  waiting for transfers between devices: 73.3 us -> 62.1 us
  local copies, waits for them, and re-layouts: 37 us -> 29.7 us
  other arithmetic: 24.2 us -> 20.9 us
    ppermute x0 -> x30, starting transfers between devices: none -> 41.1 us  [pairwise_exchange(): part = lax.ppermute(part, axis, [(d, d ^ mask) for d in range(ways)])]
    all_to_all x2 -> x0, waiting for transfers between devices: 13.8 us -> none  [one_block(): lax.all_to_all(product[None, None], 'mode', split_axis=2, concat_axis=1,...]
    all_to_all x2 -> x0, starting transfers between devices: 11.2 us -> none  [one_block(): lax.all_to_all(product[None, None], 'mode', split_axis=2, concat_axis=1,...]
    ppermute x0 -> x30, waiting for transfers between devices: none -> 11.2 us  [pairwise_exchange(): part = lax.ppermute(part, axis, [(d, d ^ mask) for d in range(ways)])]
    psum x2, waiting for transfers between devices: 45.7 us -> 38.1 us  [broadcast(): return lax.psum(block, axis)]
    while x2 -> x0, other arithmetic: 4.41 us -> none
    while x12 -> x2, local copies, waits for them, and re-layouts: 5.23 us -> 1.47 us
    all_to_all x2 -> x0, local copies, waits for them, and re-layouts: 2.98 us -> none  [one_block(): lax.all_to_all(product[None, None], 'mode', split_axis=2, concat_axis=1,...]
  transfers between devices with their start and end apart: 5 -> 33, of which waited for: 5 -> 9; matrix products, arithmetic and copies ran while one was open for 2% -> 2% of each run, Pallas kernels for 0% -> 0%
where the time goes in v1:
time: 182 us; the launch traced here: 181 us
  waiting for transfers between devices  62.1 us (34%)
  starting transfers between devices  41.2 us (23%)
  local copies, waits for them, and re-layouts  29.7 us (16%)
  other arithmetic  20.9 us (11%)
  between operations  14.9 us (8%)
  loops' own time  7.82 us (4%)
  matrix products  4.28 us (2%)
    ppermute x30, starting transfers between devices, pairwise_exchange(): part = lax.ppermute(part, axis, [(d, d ^ mask) for d in range(ways)])  41.1 us
    psum x2, waiting for transfers between devices, broadcast(): return lax.psum(block, axis)  38.1 us
    concatenate x1, other arithmetic, widen_first(): return jnp.concatenate([upper, lower], axis=0)  13.1 us
    reduce_scatter x1, waiting for transfers between devices, on_device(): lax.psum_scatter(amplitude, 'cuts', scatter_dimension=1, tiled=True)  12.8 us
    unnamed x16, local copies, waits for them, and re-layouts  12.6 us
    ppermute x30, waiting for transfers between devices, pairwise_exchange(): part = lax.ppermute(part, axis, [(d, d ^ mask) for d in range(ways)])  11.2 us
    another operation x1, loops' own time, on_device(): amplitude = lax.fori_loop(0, block_count, one_block, begin)  7.82 us
  transfers between devices with their start and end apart: 33, of which 9 were waited for; matrix products, arithmetic and copies ran while one was open for 2% of the time, Pallas kernels for 0%

profile of v1, /device:TPU:0, one launch (start us, length us, event | category | flops | bytes accessed | tf_op | source)
XLA Modules:
  0.0 181.0 jit_solution(16949929105906179372)
XLA Ops:
  7.4 3.3 %slice_bitcast_fusion.2 = (bf16[8,256,256]{2,1,0:T(8,128)(2,1)}, bf16[8,256,256]{2,1,0:T(8,128)(2,1)}) fusion(bf16[8,2,256,256]{3,2,1,0:T(8,128)(2,1)} %param.9), kind=kLoop, calls=%fused_computation.49 | loop fusion | bytes 4194304 | tf_op jit(solution)/shard_map/vmap()/squeeze | solution.py:36
  12.6 3.1 %copy.11 = bf16[8,2,256,256]{2,0,3,1:T(8,128)(2,1)} copy(bf16[8,2,256,256]{3,2,1,0:T(8,128)(2,1)S(1)} %copy-done.4) | data formatting | bytes 4194304 | tf_op args[1]
  15.7 2.4 %gather_fusion = bf16[256,8,2,256]{3,1,2,0:T(8,128)(2,1)S(1)} fusion(bf16[8,2,256,256]{2,0,3,1:T(8,128)(2,1)} %copy.11, s32[1024]{0:T(1024)S(1)} %pad_clamp_fusion), kind=kCustom, calls=%fused_computation | custom fusion | bytes 4195328 | tf_op jit(solution)/shard_map/jit(_take)/gather | solution.py:61
  20.3 13.1 %maximum_maximum_fusion = bf16[8,512,512]{1,0,2:T(8,128)(2,1)} fusion(bf16[8,256,256]{1,0,2:T(8,128)(2,1)} %get-tuple-element.174, bf16[8,256,256]{1,0,2:T(8,128)(2,1)S(1)} %fusion.6, bf16[8,256,256]{1,0,2:T(8,128)(2,1)S(1)} %get-tuple-element.173), kind=kLoop, calls=%fused_computation.42 | loop fusion | flops 16777216 | bytes 7340032 | tf_op jit(solution)/shard_map/vmap()/concatenate | solution.py:32
  33.4 7.8 %copy.16 = bf16[8,512,512]{2,1,0:T(8,128)(2,1)} copy(bf16[8,512,512]{1,0,2:T(8,128)(2,1)} %maximum_maximum_fusion) | data formatting | bytes 8388608
  41.2 2.0 %maximum_bitcast_fusion.1 = (bf16[1,8,256,512]{3,2,0,1:T(8,128)(2,1)S(1)}, bf16[1,8,256,512]{3,2,0,1:T(8,128)(2,1)S(1)}) fusion(bf16[8,256,256]{2,1,0:T(8,128)(2,1)S(1)} %copy-done.3, bf16[8,256,256]{2,1,0:T(8,128)(2,1)} %get-tuple-element.172, bf16[8,256,256]{2,1,0:T(8,128)(2,1)S(1)} %copy-done.2), kind=kLoop, calls=%fused_computation.44 | loop fusion | flops 8388608 | bytes 7340032 | tf_op jit(solution)/shard_map/vmap()/stack | solution.py:39
  43.2 2.4 %maximum_bitcast_fusion = bf16[8,2,256,512]{3,2,1,0:T(8,128)(2,1)} fusion(bf16[1,8,256,512]{3,2,0,1:T(8,128)(2,1)S(1)} %get-tuple-element.176, bf16[1,8,256,512]{3,2,0,1:T(8,128)(2,1)S(1)} %get-tuple-element.175), kind=kLoop, calls=%fused_computation.43 | loop fusion | flops 2097152 | bytes 8388608 | tf_op jit(solution)/shard_map/vmap()/transpose | solution.py:62
  45.6 112.5 %while.14 = (s32[]{:T(128)}, f32[16,16,512]{2,1,0:T(8,128)S(1)}, bf16[1,256,2,256]{3,2,1,0:T(2,128)(2,1)}, s32[2,2]{1,0:T(2,128)S(1)}, bf16[8,512,512]{2,1,0:T(8...) while((s32[]{:T(128)}, f32[16,16,512]{2,1,0:T(8,128)S(1)}, ...), condition=%wide.region_2.3_spmd.clone, body=%wide.region_0.0_spmd.clone.sunk | while | flops 269090816 | bytes 9341539 | solution.py:79
  53.0 21.7 %all-reduce.2.cloned.1.call-done = bf16[256,512]{1,0:T(8,128)(2,1)} async-done(((bf16[256,512]{1,0:T(8,128)(2,1)}), bf16[256,512]{1,0:T(8,128)(2,1)}) %all-reduce.2.cloned.1.call-update) | async-done | bytes 262160 | tf_op jit(solution)/shard_map/while/body/eval_jaxpr/psum | solution.py:25
  76.3 1.5 collective-permute-start.1
  78.2 1.5 collective-permute-start.3
  79.9 2.5 %collective-permute-start.5 = (bf16[1,1,16,512]{3,2,1,0:T(8,128)(2,1)S(1)}, bf16[1,1,16,512]{3,2,1,0:T(8,128)(2,1)S(1)}, u32[]{:S(2)}, u32[]{:S(2)}) collective-permute-start(bf16[1,1,16,512]{3,2,1,0:T(8,128)(2,1)S(1)} %get-tuple-element.237), channel_id=1, source_target_pairs={{0,6},{1,7},{2,4},{3,5},{4,2},{5,3},{6,0},{7,1},{8,14},{9,15},{10,... | collective-permute-start | bytes 49160 | tf_op jit(solution)/shard_map/while/body/eval_jaxpr/ppermute | solution.py:18
  82.7 2.4 %collective-permute-start.7 = (bf16[1,1,16,512]{3,2,1,0:T(8,128)(2,1)S(1)}, bf16[1,1,16,512]{3,2,1,0:T(8,128)(2,1)S(1)}, u32[]{:S(2)}, u32[]{:S(2)}) collective-permute-start(bf16[1,1,16,512]{3,2,1,0:T(8,128)(2,1)S(1)} %get-tuple-element.239), channel_id=1, source_target_pairs={{0,8},{1,9},{2,10},{3,11},{4,12},{5,13},{6,14},{7,15},{8,0},{9,1},... | collective-permute-start | bytes 49160 | tf_op jit(solution)/shard_map/while/body/eval_jaxpr/ppermute | solution.py:18
  85.3 3.3 %collective-permute-start.9 = (bf16[1,1,16,512]{3,2,1,0:T(8,128)(2,1)S(1)}, bf16[1,1,16,512]{3,2,1,0:T(8,128)(2,1)S(1)}, u32[]{:S(2)}, u32[]{:S(2)}) collective-permute-start(bf16[1,1,16,512]{3,2,1,0:T(8,128)(2,1)S(1)} %get-tuple-element.241), channel_id=1, source_target_pairs={{0,10},{1,11},{2,8},{3,9},{4,14},{5,15},{6,12},{7,13},{8,2},{9,3},... | collective-permute-start | bytes 49160 | tf_op jit(solution)/shard_map/while/body/eval_jaxpr/ppermute | solution.py:18
  88.9 3.3 %collective-permute-start.11 = (bf16[1,1,16,512]{3,2,1,0:T(8,128)(2,1)S(1)}, bf16[1,1,16,512]{3,2,1,0:T(8,128)(2,1)S(1)}, u32[]{:S(2)}, u32[]{:S(2)}) collective-permute-start(bf16[1,1,16,512]{3,2,1,0:T(8,128)(2,1)S(1)} %get-tuple-element.243), channel_id=1, source_target_pairs={{0,12},{1,13},{2,14},{3,15},{4,8},{5,9},{6,10},{7,11},{8,4},{9,5},... | collective-permute-start | bytes 49160 | tf_op jit(solution)/shard_map/while/body/eval_jaxpr/ppermute | solution.py:18
  92.4 4.2 %collective-permute-start.13 = (bf16[1,1,16,512]{3,2,1,0:T(8,128)(2,1)S(1)}, bf16[1,1,16,512]{3,2,1,0:T(8,128)(2,1)S(1)}, u32[]{:S(2)}, u32[]{:S(2)}) collective-permute-start(bf16[1,1,16,512]{3,2,1,0:T(8,128)(2,1)S(1)} %get-tuple-element.245), channel_id=1, source_target_pairs={{0,14},{1,15},{2,12},{3,13},{4,10},{5,11},{6,8},{7,9},{8,6},{9,7},... | collective-permute-start | bytes 49160 | tf_op jit(solution)/shard_map/while/body/eval_jaxpr/ppermute | solution.py:18
  97.3 1.6 collective-permute-done.13
  98.8 3.7 %collective-permute-done.14 = bf16[1,1,16,512]{3,2,1,0:T(8,128)(2,1)S(1)} collective-permute-done((bf16[1,1,16,512]{3,2,1,0:T(8,128)(2,1)S(1)}, bf16[1,1,16,512]{3,2,1,0:T(8,128)(2,1)S(1)}, u32[]{:S(2)}, u32[]{:S(2)}) %collective-permute-start.14) | collective-permute-done | bytes 16416 | tf_op jit(solution)/shard_map/while/body/eval_jaxpr/ppermute | solution.py:18
  102.5 1.7 reshape.105
  111.5 16.4 %all-reduce.2.cloned.1.call-done = bf16[256,512]{1,0:T(8,128)(2,1)} async-done(((bf16[256,512]{1,0:T(8,128)(2,1)}), bf16[256,512]{1,0:T(8,128)(2,1)}) %all-reduce.2.cloned.1.call-update) | async-done | bytes 262160 | tf_op jit(solution)/shard_map/while/body/eval_jaxpr/psum | solution.py:25
  129.4 1.5 collective-permute-start.1
  131.3 1.5 collective-permute-start.3
  133.0 2.5 %collective-permute-start.5 = (bf16[1,1,16,512]{3,2,1,0:T(8,128)(2,1)S(1)}, bf16[1,1,16,512]{3,2,1,0:T(8,128)(2,1)S(1)}, u32[]{:S(2)}, u32[]{:S(2)}) collective-permute-start(bf16[1,1,16,512]{3,2,1,0:T(8,128)(2,1)S(1)} %get-tuple-element.237), channel_id=1, source_target_pairs={{0,6},{1,7},{2,4},{3,5},{4,2},{5,3},{6,0},{7,1},{8,14},{9,15},{10,... | collective-permute-start | bytes 49160 | tf_op jit(solution)/shard_map/while/body/eval_jaxpr/ppermute | solution.py:18
  135.8 2.4 %collective-permute-start.7 = (bf16[1,1,16,512]{3,2,1,0:T(8,128)(2,1)S(1)}, bf16[1,1,16,512]{3,2,1,0:T(8,128)(2,1)S(1)}, u32[]{:S(2)}, u32[]{:S(2)}) collective-permute-start(bf16[1,1,16,512]{3,2,1,0:T(8,128)(2,1)S(1)} %get-tuple-element.239), channel_id=1, source_target_pairs={{0,8},{1,9},{2,10},{3,11},{4,12},{5,13},{6,14},{7,15},{8,0},{9,1},... | collective-permute-start | bytes 49160 | tf_op jit(solution)/shard_map/while/body/eval_jaxpr/ppermute | solution.py:18
  138.4 3.3 %collective-permute-start.9 = (bf16[1,1,16,512]{3,2,1,0:T(8,128)(2,1)S(1)}, bf16[1,1,16,512]{3,2,1,0:T(8,128)(2,1)S(1)}, u32[]{:S(2)}, u32[]{:S(2)}) collective-permute-start(bf16[1,1,16,512]{3,2,1,0:T(8,128)(2,1)S(1)} %get-tuple-element.241), channel_id=1, source_target_pairs={{0,10},{1,11},{2,8},{3,9},{4,14},{5,15},{6,12},{7,13},{8,2},{9,3},... | collective-permute-start | bytes 49160 | tf_op jit(solution)/shard_map/while/body/eval_jaxpr/ppermute | solution.py:18
  142.0 3.3 %collective-permute-start.11 = (bf16[1,1,16,512]{3,2,1,0:T(8,128)(2,1)S(1)}, bf16[1,1,16,512]{3,2,1,0:T(8,128)(2,1)S(1)}, u32[]{:S(2)}, u32[]{:S(2)}) collective-permute-start(bf16[1,1,16,512]{3,2,1,0:T(8,128)(2,1)S(1)} %get-tuple-element.243), channel_id=1, source_target_pairs={{0,12},{1,13},{2,14},{3,15},{4,8},{5,9},{6,10},{7,11},{8,4},{9,5},... | collective-permute-start | bytes 49160 | tf_op jit(solution)/shard_map/while/body/eval_jaxpr/ppermute | solution.py:18
  145.5 4.2 %collective-permute-start.13 = (bf16[1,1,16,512]{3,2,1,0:T(8,128)(2,1)S(1)}, bf16[1,1,16,512]{3,2,1,0:T(8,128)(2,1)S(1)}, u32[]{:S(2)}, u32[]{:S(2)}) collective-permute-start(bf16[1,1,16,512]{3,2,1,0:T(8,128)(2,1)S(1)} %get-tuple-element.245), channel_id=1, source_target_pairs={{0,14},{1,15},{2,12},{3,13},{4,10},{5,11},{6,8},{7,9},{8,6},{9,7},... | collective-permute-start | bytes 49160 | tf_op jit(solution)/shard_map/while/body/eval_jaxpr/ppermute | solution.py:18
  150.4 1.6 collective-permute-done.13
  152.0 3.7 %collective-permute-done.14 = bf16[1,1,16,512]{3,2,1,0:T(8,128)(2,1)S(1)} collective-permute-done((bf16[1,1,16,512]{3,2,1,0:T(8,128)(2,1)S(1)}, bf16[1,1,16,512]{3,2,1,0:T(8,128)(2,1)S(1)}, u32[]{:S(2)}, u32[]{:S(2)}) %collective-permute-start.14) | collective-permute-done | bytes 16416 | tf_op jit(solution)/shard_map/while/body/eval_jaxpr/ppermute | solution.py:18
  155.6 1.7 reshape.105
  158.9 12.8 %reduce-scatter.2.cloned.1.call-done = f32[16,8,512]{2,1,0:T(8,128)} async-done(((f32[16,16,512]{2,1,0:T(8,128)}), f32[16,8,512]{2,1,0:T(8,128)}) %reduce-scatter.2.cloned.1.call-update) | async-done | bytes 262160 | tf_op jit(solution)/shard_map/reduce_scatter | solution.py:80
  171.7 1.8 %reshape.88 = f32[16,8,2,256]{3,2,1,0:T(2,128)} reshape(f32[16,8,512]{2,1,0:T(8,128)} %reduce-scatter.2.cloned.1.call-done) | data formatting | bytes 524288 | tf_op jit(solution)/shard_map/reshape | solution.py:81
  (120 shorter events, 20.2 us)
Async XLA Ops:
  45.6 29.1 %all-reduce.2.cloned.1.call-start = ((), (), s32[]{:S(2)}) async-start(), calls=%async_computation.2 | async-start | bytes 524288 | tf_op jit(solution)/shard_map/while/body/eval_jaxpr/psum | solution.py:25
  76.2 3.7 %collective-permute-start = (bf16[1,1,16,512]{3,2,1,0:T(8,128)(2,1)S(1)}, bf16[1,1,16,512]{3,2,1,0:T(8,128)(2,1)S(1)}, u32[]{:S(2)}, u32[]{:S(2)}) collective-permute-start(bf16[1,1,16,512]{3,2,1,0:T(8,128)(2,1)S(1)} %get-tuple-element.232), channel_id=1, source_target_pairs={{0,1},{1,0},{2,3},{3,2},{4,5},{5,4},{6,7},{7,6},{8,9},{9,8},{10,11... | collective-permute-start | bytes 49160 | tf_op jit(solution)/shard_map/while/body/eval_jaxpr/ppermute | solution.py:18
  76.3 6.1 %collective-permute-start.1 = (bf16[1,1,16,512]{3,2,1,0:T(8,128)(2,1)S(1)}, bf16[1,1,16,512]{3,2,1,0:T(8,128)(2,1)S(1)}, u32[]{:S(2)}, u32[]{:S(2)}) collective-permute-start(bf16[1,1,16,512]{3,2,1,0:T(8,128)(2,1)S(1)} %get-tuple-element.233), channel_id=1, source_target_pairs={{0,2},{1,3},{2,0},{3,1},{4,6},{5,7},{6,4},{7,5},{8,10},{9,11},{10,... | collective-permute-start | bytes 49160 | tf_op jit(solution)/shard_map/while/body/eval_jaxpr/ppermute | solution.py:18
  77.8 4.9 %collective-permute-start.2 = (bf16[1,1,16,512]{3,2,1,0:T(8,128)(2,1)S(1)}, bf16[1,1,16,512]{3,2,1,0:T(8,128)(2,1)S(1)}, u32[]{:S(2)}, u32[]{:S(2)}) collective-permute-start(bf16[1,1,16,512]{3,2,1,0:T(8,128)(2,1)S(1)} %get-tuple-element.234), channel_id=1, source_target_pairs={{0,3},{1,2},{2,1},{3,0},{4,7},{5,6},{6,5},{7,4},{8,11},{9,10},{10,... | collective-permute-start | bytes 49160 | tf_op jit(solution)/shard_map/while/body/eval_jaxpr/ppermute | solution.py:18
  78.2 6.9 %collective-permute-start.3 = (bf16[1,1,16,512]{3,2,1,0:T(8,128)(2,1)S(1)}, bf16[1,1,16,512]{3,2,1,0:T(8,128)(2,1)S(1)}, u32[]{:S(2)}, u32[]{:S(2)}) collective-permute-start(bf16[1,1,16,512]{3,2,1,0:T(8,128)(2,1)S(1)} %get-tuple-element.235), channel_id=1, source_target_pairs={{0,4},{1,5},{2,6},{3,7},{4,0},{5,1},{6,2},{7,3},{8,12},{9,13},{10,... | collective-permute-start | bytes 49160 | tf_op jit(solution)/shard_map/while/body/eval_jaxpr/ppermute | solution.py:18
  79.6 5.7 %collective-permute-start.4 = (bf16[1,1,16,512]{3,2,1,0:T(8,128)(2,1)S(1)}, bf16[1,1,16,512]{3,2,1,0:T(8,128)(2,1)S(1)}, u32[]{:S(2)}, u32[]{:S(2)}) collective-permute-start(bf16[1,1,16,512]{3,2,1,0:T(8,128)(2,1)S(1)} %get-tuple-element.236), channel_id=1, source_target_pairs={{0,5},{1,4},{2,7},{3,6},{4,1},{5,0},{6,3},{7,2},{8,13},{9,12},{10,... | collective-permute-start | bytes 49160 | tf_op jit(solution)/shard_map/while/body/eval_jaxpr/ppermute | solution.py:18
  79.9 8.7 %collective-permute-start.5 = (bf16[1,1,16,512]{3,2,1,0:T(8,128)(2,1)S(1)}, bf16[1,1,16,512]{3,2,1,0:T(8,128)(2,1)S(1)}, u32[]{:S(2)}, u32[]{:S(2)}) collective-permute-start(bf16[1,1,16,512]{3,2,1,0:T(8,128)(2,1)S(1)} %get-tuple-element.237), channel_id=1, source_target_pairs={{0,6},{1,7},{2,4},{3,5},{4,2},{5,3},{6,0},{7,1},{8,14},{9,15},{10,... | collective-permute-start | bytes 49160 | tf_op jit(solution)/shard_map/while/body/eval_jaxpr/ppermute | solution.py:18
  82.4 6.5 %collective-permute-start.6 = (bf16[1,1,16,512]{3,2,1,0:T(8,128)(2,1)S(1)}, bf16[1,1,16,512]{3,2,1,0:T(8,128)(2,1)S(1)}, u32[]{:S(2)}, u32[]{:S(2)}) collective-permute-start(bf16[1,1,16,512]{3,2,1,0:T(8,128)(2,1)S(1)} %get-tuple-element.238), channel_id=1, source_target_pairs={{0,7},{1,6},{2,5},{3,4},{4,3},{5,2},{6,1},{7,0},{8,15},{9,14},{10,... | collective-permute-start | bytes 49160 | tf_op jit(solution)/shard_map/while/body/eval_jaxpr/ppermute | solution.py:18
  82.7 9.6 %collective-permute-start.7 = (bf16[1,1,16,512]{3,2,1,0:T(8,128)(2,1)S(1)}, bf16[1,1,16,512]{3,2,1,0:T(8,128)(2,1)S(1)}, u32[]{:S(2)}, u32[]{:S(2)}) collective-permute-start(bf16[1,1,16,512]{3,2,1,0:T(8,128)(2,1)S(1)} %get-tuple-element.239), channel_id=1, source_target_pairs={{0,8},{1,9},{2,10},{3,11},{4,12},{5,13},{6,14},{7,15},{8,0},{9,1},... | collective-permute-start | bytes 49160 | tf_op jit(solution)/shard_map/while/body/eval_jaxpr/ppermute | solution.py:18
  85.1 7.3 %collective-permute-start.8 = (bf16[1,1,16,512]{3,2,1,0:T(8,128)(2,1)S(1)}, bf16[1,1,16,512]{3,2,1,0:T(8,128)(2,1)S(1)}, u32[]{:S(2)}, u32[]{:S(2)}) collective-permute-start(bf16[1,1,16,512]{3,2,1,0:T(8,128)(2,1)S(1)} %get-tuple-element.240), channel_id=1, source_target_pairs={{0,9},{1,8},{2,11},{3,10},{4,13},{5,12},{6,15},{7,14},{8,1},{9,0},... | collective-permute-start | bytes 49160 | tf_op jit(solution)/shard_map/while/body/eval_jaxpr/ppermute | solution.py:18
  85.3 11.4 %collective-permute-start.9 = (bf16[1,1,16,512]{3,2,1,0:T(8,128)(2,1)S(1)}, bf16[1,1,16,512]{3,2,1,0:T(8,128)(2,1)S(1)}, u32[]{:S(2)}, u32[]{:S(2)}) collective-permute-start(bf16[1,1,16,512]{3,2,1,0:T(8,128)(2,1)S(1)} %get-tuple-element.241), channel_id=1, source_target_pairs={{0,10},{1,11},{2,8},{3,9},{4,14},{5,15},{6,12},{7,13},{8,2},{9,3},... | collective-permute-start | bytes 49160 | tf_op jit(solution)/shard_map/while/body/eval_jaxpr/ppermute | solution.py:18
  88.6 8.3 %collective-permute-start.10 = (bf16[1,1,16,512]{3,2,1,0:T(8,128)(2,1)S(1)}, bf16[1,1,16,512]{3,2,1,0:T(8,128)(2,1)S(1)}, u32[]{:S(2)}, u32[]{:S(2)}) collective-permute-start(bf16[1,1,16,512]{3,2,1,0:T(8,128)(2,1)S(1)} %get-tuple-element.242), channel_id=1, source_target_pairs={{0,11},{1,10},{2,9},{3,8},{4,15},{5,14},{6,13},{7,12},{8,3},{9,2},... | collective-permute-start | bytes 49160 | tf_op jit(solution)/shard_map/while/body/eval_jaxpr/ppermute | solution.py:18
  88.9 8.0 %collective-permute-start.11 = (bf16[1,1,16,512]{3,2,1,0:T(8,128)(2,1)S(1)}, bf16[1,1,16,512]{3,2,1,0:T(8,128)(2,1)S(1)}, u32[]{:S(2)}, u32[]{:S(2)}) collective-permute-start(bf16[1,1,16,512]{3,2,1,0:T(8,128)(2,1)S(1)} %get-tuple-element.243), channel_id=1, source_target_pairs={{0,12},{1,13},{2,14},{3,15},{4,8},{5,9},{6,10},{7,11},{8,4},{9,5},... | collective-permute-start | bytes 49160 | tf_op jit(solution)/shard_map/while/body/eval_jaxpr/ppermute | solution.py:18
  92.2 5.0 %collective-permute-start.12 = (bf16[1,1,16,512]{3,2,1,0:T(8,128)(2,1)S(1)}, bf16[1,1,16,512]{3,2,1,0:T(8,128)(2,1)S(1)}, u32[]{:S(2)}, u32[]{:S(2)}) collective-permute-start(bf16[1,1,16,512]{3,2,1,0:T(8,128)(2,1)S(1)} %get-tuple-element.244), channel_id=1, source_target_pairs={{0,13},{1,12},{2,15},{3,14},{4,9},{5,8},{6,11},{7,10},{8,5},{9,4},... | collective-permute-start | bytes 49160 | tf_op jit(solution)/shard_map/while/body/eval_jaxpr/ppermute | solution.py:18
  92.4 6.4 %collective-permute-start.13 = (bf16[1,1,16,512]{3,2,1,0:T(8,128)(2,1)S(1)}, bf16[1,1,16,512]{3,2,1,0:T(8,128)(2,1)S(1)}, u32[]{:S(2)}, u32[]{:S(2)}) collective-permute-start(bf16[1,1,16,512]{3,2,1,0:T(8,128)(2,1)S(1)} %get-tuple-element.245), channel_id=1, source_target_pairs={{0,14},{1,15},{2,12},{3,13},{4,10},{5,11},{6,8},{7,9},{8,6},{9,7},... | collective-permute-start | bytes 49160 | tf_op jit(solution)/shard_map/while/body/eval_jaxpr/ppermute | solution.py:18
  96.7 5.9 %collective-permute-start.14 = (bf16[1,1,16,512]{3,2,1,0:T(8,128)(2,1)S(1)}, bf16[1,1,16,512]{3,2,1,0:T(8,128)(2,1)S(1)}, u32[]{:S(2)}, u32[]{:S(2)}) collective-permute-start(bf16[1,1,16,512]{3,2,1,0:T(8,128)(2,1)S(1)} %get-tuple-element.246), channel_id=1, source_target_pairs={{0,15},{1,14},{2,13},{3,12},{4,11},{5,10},{6,9},{7,8},{8,7},{9,6},... | collective-permute-start | bytes 49160 | tf_op jit(solution)/shard_map/while/body/eval_jaxpr/ppermute | solution.py:18
  104.9 22.9 %all-reduce.2.cloned.1.call-start = ((), (), s32[]{:S(2)}) async-start(), calls=%async_computation.2 | async-start | bytes 524288 | tf_op jit(solution)/shard_map/while/body/eval_jaxpr/psum | solution.py:25
  129.4 6.1 %collective-permute-start.1 = (bf16[1,1,16,512]{3,2,1,0:T(8,128)(2,1)S(1)}, bf16[1,1,16,512]{3,2,1,0:T(8,128)(2,1)S(1)}, u32[]{:S(2)}, u32[]{:S(2)}) collective-permute-start(bf16[1,1,16,512]{3,2,1,0:T(8,128)(2,1)S(1)} %get-tuple-element.233), channel_id=1, source_target_pairs={{0,2},{1,3},{2,0},{3,1},{4,6},{5,7},{6,4},{7,5},{8,10},{9,11},{10,... | collective-permute-start | bytes 49160 | tf_op jit(solution)/shard_map/while/body/eval_jaxpr/ppermute | solution.py:18
  131.0 4.9 %collective-permute-start.2 = (bf16[1,1,16,512]{3,2,1,0:T(8,128)(2,1)S(1)}, bf16[1,1,16,512]{3,2,1,0:T(8,128)(2,1)S(1)}, u32[]{:S(2)}, u32[]{:S(2)}) collective-permute-start(bf16[1,1,16,512]{3,2,1,0:T(8,128)(2,1)S(1)} %get-tuple-element.234), channel_id=1, source_target_pairs={{0,3},{1,2},{2,1},{3,0},{4,7},{5,6},{6,5},{7,4},{8,11},{9,10},{10,... | collective-permute-start | bytes 49160 | tf_op jit(solution)/shard_map/while/body/eval_jaxpr/ppermute | solution.py:18
  131.3 6.9 %collective-permute-start.3 = (bf16[1,1,16,512]{3,2,1,0:T(8,128)(2,1)S(1)}, bf16[1,1,16,512]{3,2,1,0:T(8,128)(2,1)S(1)}, u32[]{:S(2)}, u32[]{:S(2)}) collective-permute-start(bf16[1,1,16,512]{3,2,1,0:T(8,128)(2,1)S(1)} %get-tuple-element.235), channel_id=1, source_target_pairs={{0,4},{1,5},{2,6},{3,7},{4,0},{5,1},{6,2},{7,3},{8,12},{9,13},{10,... | collective-permute-start | bytes 49160 | tf_op jit(solution)/shard_map/while/body/eval_jaxpr/ppermute | solution.py:18
  132.8 5.7 %collective-permute-start.4 = (bf16[1,1,16,512]{3,2,1,0:T(8,128)(2,1)S(1)}, bf16[1,1,16,512]{3,2,1,0:T(8,128)(2,1)S(1)}, u32[]{:S(2)}, u32[]{:S(2)}) collective-permute-start(bf16[1,1,16,512]{3,2,1,0:T(8,128)(2,1)S(1)} %get-tuple-element.236), channel_id=1, source_target_pairs={{0,5},{1,4},{2,7},{3,6},{4,1},{5,0},{6,3},{7,2},{8,13},{9,12},{10,... | collective-permute-start | bytes 49160 | tf_op jit(solution)/shard_map/while/body/eval_jaxpr/ppermute | solution.py:18
  133.0 8.7 %collective-permute-start.5 = (bf16[1,1,16,512]{3,2,1,0:T(8,128)(2,1)S(1)}, bf16[1,1,16,512]{3,2,1,0:T(8,128)(2,1)S(1)}, u32[]{:S(2)}, u32[]{:S(2)}) collective-permute-start(bf16[1,1,16,512]{3,2,1,0:T(8,128)(2,1)S(1)} %get-tuple-element.237), channel_id=1, source_target_pairs={{0,6},{1,7},{2,4},{3,5},{4,2},{5,3},{6,0},{7,1},{8,14},{9,15},{10,... | collective-permute-start | bytes 49160 | tf_op jit(solution)/shard_map/while/body/eval_jaxpr/ppermute | solution.py:18
  135.5 6.5 %collective-permute-start.6 = (bf16[1,1,16,512]{3,2,1,0:T(8,128)(2,1)S(1)}, bf16[1,1,16,512]{3,2,1,0:T(8,128)(2,1)S(1)}, u32[]{:S(2)}, u32[]{:S(2)}) collective-permute-start(bf16[1,1,16,512]{3,2,1,0:T(8,128)(2,1)S(1)} %get-tuple-element.238), channel_id=1, source_target_pairs={{0,7},{1,6},{2,5},{3,4},{4,3},{5,2},{6,1},{7,0},{8,15},{9,14},{10,... | collective-permute-start | bytes 49160 | tf_op jit(solution)/shard_map/while/body/eval_jaxpr/ppermute | solution.py:18
  135.8 9.6 %collective-permute-start.7 = (bf16[1,1,16,512]{3,2,1,0:T(8,128)(2,1)S(1)}, bf16[1,1,16,512]{3,2,1,0:T(8,128)(2,1)S(1)}, u32[]{:S(2)}, u32[]{:S(2)}) collective-permute-start(bf16[1,1,16,512]{3,2,1,0:T(8,128)(2,1)S(1)} %get-tuple-element.239), channel_id=1, source_target_pairs={{0,8},{1,9},{2,10},{3,11},{4,12},{5,13},{6,14},{7,15},{8,0},{9,1},... | collective-permute-start | bytes 49160 | tf_op jit(solution)/shard_map/while/body/eval_jaxpr/ppermute | solution.py:18
  138.2 7.3 %collective-permute-start.8 = (bf16[1,1,16,512]{3,2,1,0:T(8,128)(2,1)S(1)}, bf16[1,1,16,512]{3,2,1,0:T(8,128)(2,1)S(1)}, u32[]{:S(2)}, u32[]{:S(2)}) collective-permute-start(bf16[1,1,16,512]{3,2,1,0:T(8,128)(2,1)S(1)} %get-tuple-element.240), channel_id=1, source_target_pairs={{0,9},{1,8},{2,11},{3,10},{4,13},{5,12},{6,15},{7,14},{8,1},{9,0},... | collective-permute-start | bytes 49160 | tf_op jit(solution)/shard_map/while/body/eval_jaxpr/ppermute | solution.py:18
  138.4 11.4 %collective-permute-start.9 = (bf16[1,1,16,512]{3,2,1,0:T(8,128)(2,1)S(1)}, bf16[1,1,16,512]{3,2,1,0:T(8,128)(2,1)S(1)}, u32[]{:S(2)}, u32[]{:S(2)}) collective-permute-start(bf16[1,1,16,512]{3,2,1,0:T(8,128)(2,1)S(1)} %get-tuple-element.241), channel_id=1, source_target_pairs={{0,10},{1,11},{2,8},{3,9},{4,14},{5,15},{6,12},{7,13},{8,2},{9,3},... | collective-permute-start | bytes 49160 | tf_op jit(solution)/shard_map/while/body/eval_jaxpr/ppermute | solution.py:18
  141.7 8.3 %collective-permute-start.10 = (bf16[1,1,16,512]{3,2,1,0:T(8,128)(2,1)S(1)}, bf16[1,1,16,512]{3,2,1,0:T(8,128)(2,1)S(1)}, u32[]{:S(2)}, u32[]{:S(2)}) collective-permute-start(bf16[1,1,16,512]{3,2,1,0:T(8,128)(2,1)S(1)} %get-tuple-element.242), channel_id=1, source_target_pairs={{0,11},{1,10},{2,9},{3,8},{4,15},{5,14},{6,13},{7,12},{8,3},{9,2},... | collective-permute-start | bytes 49160 | tf_op jit(solution)/shard_map/while/body/eval_jaxpr/ppermute | solution.py:18
  142.0 8.0 %collective-permute-start.11 = (bf16[1,1,16,512]{3,2,1,0:T(8,128)(2,1)S(1)}, bf16[1,1,16,512]{3,2,1,0:T(8,128)(2,1)S(1)}, u32[]{:S(2)}, u32[]{:S(2)}) collective-permute-start(bf16[1,1,16,512]{3,2,1,0:T(8,128)(2,1)S(1)} %get-tuple-element.243), channel_id=1, source_target_pairs={{0,12},{1,13},{2,14},{3,15},{4,8},{5,9},{6,10},{7,11},{8,4},{9,5},... | collective-permute-start | bytes 49160 | tf_op jit(solution)/shard_map/while/body/eval_jaxpr/ppermute | solution.py:18
  145.4 5.0 %collective-permute-start.12 = (bf16[1,1,16,512]{3,2,1,0:T(8,128)(2,1)S(1)}, bf16[1,1,16,512]{3,2,1,0:T(8,128)(2,1)S(1)}, u32[]{:S(2)}, u32[]{:S(2)}) collective-permute-start(bf16[1,1,16,512]{3,2,1,0:T(8,128)(2,1)S(1)} %get-tuple-element.244), channel_id=1, source_target_pairs={{0,13},{1,12},{2,15},{3,14},{4,9},{5,8},{6,11},{7,10},{8,5},{9,4},... | collective-permute-start | bytes 49160 | tf_op jit(solution)/shard_map/while/body/eval_jaxpr/ppermute | solution.py:18
  145.5 6.4 %collective-permute-start.13 = (bf16[1,1,16,512]{3,2,1,0:T(8,128)(2,1)S(1)}, bf16[1,1,16,512]{3,2,1,0:T(8,128)(2,1)S(1)}, u32[]{:S(2)}, u32[]{:S(2)}) collective-permute-start(bf16[1,1,16,512]{3,2,1,0:T(8,128)(2,1)S(1)} %get-tuple-element.245), channel_id=1, source_target_pairs={{0,14},{1,15},{2,12},{3,13},{4,10},{5,11},{6,8},{7,9},{8,6},{9,7},... | collective-permute-start | bytes 49160 | tf_op jit(solution)/shard_map/while/body/eval_jaxpr/ppermute | solution.py:18
  149.8 5.9 %collective-permute-start.14 = (bf16[1,1,16,512]{3,2,1,0:T(8,128)(2,1)S(1)}, bf16[1,1,16,512]{3,2,1,0:T(8,128)(2,1)S(1)}, u32[]{:S(2)}, u32[]{:S(2)}) collective-permute-start(bf16[1,1,16,512]{3,2,1,0:T(8,128)(2,1)S(1)} %get-tuple-element.246), channel_id=1, source_target_pairs={{0,15},{1,14},{2,13},{3,12},{4,11},{5,10},{6,9},{7,8},{8,7},{9,6},... | collective-permute-start | bytes 49160 | tf_op jit(solution)/shard_map/while/body/eval_jaxpr/ppermute | solution.py:18
  158.1 13.7 %reduce-scatter.2.cloned.1.call-start = ((), (), s32[]{:S(2)}) async-start(), calls=%async_computation.1 | async-start | bytes 786432 | tf_op jit(solution)/shard_map/reduce_scatter | solution.py:80
  (8 other events, 32.1 us)
Sparse Core Ops, SparseCore 0:
  48.8 25.8 all-reduce.1
  108.1 19.6 all-reduce.1
Sparse Core Ops, SparseCore 1:
  160.8 10.9 reduce-scatter.1
